TPU v7x, 256 devices: a whole 4x4x8 slice. The times are simulated.
256 devices in a mesh: section: 16 (over x, z_lo), expert: 16 (over y, z_hi, core).
Axes of the slice: x: 4, y: 4, z: 8 (z_hi: 2, z_lo: 4; z = z_hi * 4 + z_lo), core: 2. Of those that a mesh axis runs over, the one named last changes fastest.
Arguments:
- stream: bfloat16 [16, 256, 4096], P('section', 'expert'), may hold values from -6 to 6
- queries: bfloat16 [16, 256, 4096], P('section', None, 'expert'), may hold values from -6 to 6
- keyvals: bfloat16 [16, 4096, 512], P('section', 'expert'), may hold values from -6 to 6
- w_out: bfloat16 [16, 4096, 4096], P('section', 'expert'), may hold values from -0.5 to 0.5
- norm_gain: float32 [16, 4096], P('section'), may hold values from 0.5 to 1.5
- w_gate: bfloat16 [16, 4096, 6144], P('section', None, 'expert'), may hold values from -0.09375 to 0.09375
- w_up: bfloat16 [16, 4096, 6144], P('section', None, 'expert'), may hold values from -0.09375 to 0.09375
- w_down: bfloat16 [16, 6144, 4096], P('section', 'expert'), may hold values from -0.3125 to 0.3125
- routes: int32 [16, 256, 2], P('section'), may hold values from 0 to 3, all different within a row; in each aligned block of 16 rows (0 to 15, 16 to 31, ..., all dimensions but the last counted through in order) at most 12 rows name the same one
- gate_scores: float32 [16, 256, 2], P('section'), may hold values from 0.05 to 20
Outputs:
- passed: bfloat16 [16, 256, 4096], P('section', 'expert')
Inputs may be any that keep to these rules, and one draw needn't show every extreme that they name: `routes`: each row names 2 different experts. In each aligned block of 16 rows (the tokens of one device) no expert is named by more than 12 rows.
All inputs are finite; a program needn't handle non-finite values.
Results may differ from a plain program's by a relative error of at most 0.02.
Values may be sent and summed in bfloat16 or wider, within the bound.
No kernel may reach another device: no remote copies, remote signals or barrier semaphores. Data moves between devices by JAX's collectives and lax.ppermute only.
A program may use at most 64 MiB of HBM per device.

v0:
```python
import math
import jax
import jax.numpy as jnp
from jax import lax
from jax.sharding import PartitionSpec as P

HD = 128
FF = 1536
QHEADS = 32
KVHEADS = 2
CTX = 4096
MB = 256


def shifted(block, axis, distance):
    devices = range(lax.axis_size(axis))
    route = [((i - distance) % len(devices), i) for i in devices]
    return lax.ppermute(block, axis, route)


def body(stream, queries, keyvals, w_out, norm_gain, w_gate, w_up, w_down, routes, gate_scores):
    my_index = lax.axis_index("expert")
    devices = lax.axis_size("expert")
    tok_rows = stream.shape[1]
    residual = stream[0]
    query_all = queries[0]
    proj_out = w_out[0]
    gain = norm_gain[0]
    gate_w = w_gate[0]
    up_w = w_up[0]
    down_w = w_down[0]
    heads_here = query_all.shape[1] // HD
    group = QHEADS // KVHEADS
    scale = 1.0 / math.sqrt(HD)
    query_pos = CTX - MB + jnp.arange(MB, dtype=jnp.int32)
    piece = lax.all_gather(keyvals[0], "expert", axis=0, tiled=True)
    tops = jnp.full((heads_here, MB), -1e30, jnp.float32)
    totals = jnp.zeros((heads_here, MB), jnp.float32)
    sums = jnp.zeros((heads_here, MB, HD), jnp.float32)
    key_pos = jnp.arange(piece.shape[0], dtype=jnp.int32)
    visible = key_pos[None, :] <= query_pos[:, None]
    new_tops = []
    new_totals = []
    new_sums = []
    for head in range(heads_here):
        column = (my_index * heads_here + head) // group * (2 * HD)
        keys = lax.dynamic_slice_in_dim(piece, column, HD, 1)
        values = lax.dynamic_slice_in_dim(piece, column + HD, HD, 1)
        query = query_all[:, head * HD : (head + 1) * HD]
        score = (
            lax.dot_general(
                query, keys, (((1,), (1,)), ((), ())), preferred_element_type=jnp.float32
            )
            * scale
        )
        top_new = jnp.maximum(tops[head], jnp.max(jnp.where(visible, score, -1e30), axis=1))
        weight = jnp.where(visible, jnp.exp(score - top_new[:, None]), 0.0)
        factor = jnp.exp(tops[head] - top_new)
        new_tops.append(top_new)
        new_totals.append(totals[head] * factor + jnp.sum(weight, axis=1))
        new_sums.append(
            sums[head] * factor[:, None]
            + jnp.dot(weight.astype(jnp.bfloat16), values, preferred_element_type=jnp.float32)
        )
    totals = jnp.stack(new_totals)
    sums = jnp.stack(new_sums)
    heads = (sums / totals[:, :, None]).astype(jnp.bfloat16)
    heads = jnp.transpose(heads, (1, 0, 2)).reshape(MB, heads_here * HD)
    attended = lax.psum_scatter(
        jnp.dot(heads, proj_out, preferred_element_type=jnp.float32).astype(jnp.bfloat16),
        "expert",
        scatter_dimension=0,
        tiled=True,
    ).astype(jnp.float32)
    middle = residual.astype(jnp.float32) + attended
    normed = (
        middle * lax.rsqrt(jnp.mean(middle * middle, axis=1, keepdims=True) + 1e-06) * gain
    ).astype(jnp.bfloat16)
    split = FF // gate_w.shape[1]
    experts_count = devices // split
    chosen = lax.dynamic_slice_in_dim(routes[0], my_index * tok_rows, tok_rows, 0)
    scores_in = lax.dynamic_slice_in_dim(gate_scores[0], my_index * tok_rows, tok_rows, 0)
    onehot = chosen[:, :, None] == jnp.arange(experts_count, dtype=jnp.int32)[None, None, :]
    share = jnp.sum(jnp.where(onehot, scores_in[:, :, None], 0.0), axis=1) / jnp.sum(
        scores_in, axis=1, keepdims=True
    )
    share_dev = jnp.repeat(share, split, axis=1)
    outgoing_rows = jnp.broadcast_to(normed[None], (devices, tok_rows, normed.shape[1]))
    rows = lax.all_to_all(outgoing_rows, "expert", split_axis=0, concat_axis=0, tiled=True)
    flat = rows.reshape(-1, rows.shape[-1])
    gate = jnp.dot(flat, gate_w, preferred_element_type=jnp.float32)
    upper = jnp.dot(flat, up_w, preferred_element_type=jnp.float32)
    activated = (jax.nn.silu(gate) * upper).astype(jnp.bfloat16)
    computed = (
        jnp.dot(activated, down_w, preferred_element_type=jnp.float32)
        .astype(jnp.bfloat16)
        .reshape(rows.shape)
    )
    picked = lax.all_to_all(computed, "expert", split_axis=0, concat_axis=0, tiled=True)
    mixed = jnp.einsum(
        "td,dtk->tk", share_dev, picked.astype(jnp.float32), precision=lax.Precision.HIGHEST
    )
    layer_out = (middle + mixed).astype(jnp.bfloat16)
    return shifted(layer_out[None], "section", 1)


def solution(mesh):
    return jax.shard_map(
        body,
        mesh=mesh,
        in_specs=(
            P("section", "expert", None),
            P("section", None, "expert"),
            P("section", "expert", None),
            P("section", "expert", None),
            P("section", None),
            P("section", None, "expert"),
            P("section", None, "expert"),
            P("section", "expert", None),
            P("section", None, None),
            P("section", None, None),
        ),
        out_specs=P("section", "expert", None),
        check_vma=False,
    )
```

profile of v0, /device:TPU:8, one launch (start us, length us, event | category | flops | bytes accessed | tf_op | source)
XLA Modules:
  0.0 325.5 jit_solution(16367630738279816033)
XLA Ops:
  6.5 0.0 copy-start
  6.5 0.0 copy-start.10
  6.5 0.0 all-gather.3.cloned.1.call-start
  6.5 0.7 all-gather.3.cloned.1.call-update
  7.3 0.0 reduce-scatter.2.cloned.1.call-start
  7.4 82.3 %all-gather.3.cloned.1.call-done = bf16[1,4096,512]{2,1,0:T(8,128)(2,1)} async-done(((bf16[1,256,512]{2,1,0:T(8,128)(2,1)}), bf16[1,4096,512]{2,1,0:T(8,128)(2,1)}) %all-gather.3.cloned.1.call-update) | async-done | bytes 4194320 | tf_op jit(solution)/shard_map/all_gather | solution.py:36
  89.7 0.0 copy-start.8
  89.7 2.3 select_reduce_fusion.1
  92.0 0.0 copy-done.10
  92.0 0.2 copy-done.8
  92.2 1.7 fusion.2
  93.9 1.1 fusion.4
  95.0 1.0 fusion.27
  96.1 0.0 copy-start.1
  96.1 1.0 fusion.33
  97.1 0.0 copy-start.3
  97.1 0.0 copy-start.5
  97.1 0.5 copy-done.1
  97.6 2.1 convolution_convert_fusion.1
  99.7 0.0 reduce-scatter.2.cloned.1.call-update
  99.7 83.5 %reduce-scatter.2.cloned.1.call-done = bf16[16,4096]{1,0:T(8,128)(2,1)} async-done(((bf16[256,4096]{1,0:T(8,128)(2,1)}), bf16[16,4096]{1,0:T(8,128)(2,1)}) %reduce-scatter.2.cloned.1.call-update) | async-done | bytes 131088 | tf_op jit(solution)/shard_map/reduce_scatter | solution.py:69
  183.3 0.0 copy-done.3
  183.3 0.0 copy-start.9
  183.3 1.2 multiply_reduce_fusion
  184.5 0.0 copy-done.5
  184.5 1.0 multiply_convert_fusion
  185.5 0.2 broadcast_in_dim.53
  185.8 34.0 %all_to_all.10 = bf16[16,16,4096]{2,1,0:T(8,128)(2,1)S(1)} all-to-all(bf16[16,16,4096]{2,1,0:T(8,128)(2,1)S(1)} %broadcast_in_dim.53), channel_id=1, replica_groups=mesh['section'=16,'expert'=16] {'expert'}, dimensions={0} | all-to-all | bytes 4194304 | tf_op jit(solution)/shard_map/all_to_all | solution.py:89
  219.8 0.0 copy-start.2
  219.8 1.3 copy-done.2
  221.1 0.0 copy-done.9
  221.1 2.0 fusion.9
  223.1 0.0 copy-done
  223.1 6.4 %convolution_convert_fusion = bf16[256,4096]{1,0:T(8,128)(2,1)} fusion(bf16[1,384,4096]{2,1,0:T(8,128)(2,1)S(1)} %copy-done, bf16[256,4096]{1,0:T(8,128)(2,1)} %bitcast.77, bf16[1,4096,384]{2,1,0:T(8,128)(2,1)} %param.16, f32[256,384]{1,0:T(8,128)} %fusion.9), kind=kOutput, calls=%fused_computation.4 | convolution fusion | flops 1612251136 | bytes 10878976 | tf_op jit(solution)/shard_map/dot_general | solution.py:95
  229.5 0.0 copy-start.6
  229.5 7.2 %all-to-all-start.1 = ((bf16[16,16,4096]{2,1,0:T(8,128)(2,1)}), bf16[16,16,4096]{2,1,0:T(8,128)(2,1)}, u32[]{:S(2)}, u32[]{:S(2)}) async-start(bf16[16,16,4096]{2,1,0:T(8,128)(2,1)} %bitcast.75), calls=%async_computation.2 | async-start | bytes 4194304 | tf_op jit(solution)/shard_map/all_to_all | solution.py:99
  236.7 0.0 copy-done.6
  236.7 0.1 fusion.62
  236.8 0.0 copy-done.7
  236.8 0.1 fusion.61
  236.9 0.1 copy.15
  236.9 29.0 %all-to-all-done.1 = bf16[16,16,4096]{2,1,0:T(8,128)(2,1)} async-done(((bf16[16,16,4096]{2,1,0:T(8,128)(2,1)}), bf16[16,16,4096]{2,1,0:T(8,128)(2,1)}, u32[]{:S(2)}, u32[]{:S(2)}) %all-to-all-start.1) | async-done | bytes 2097184 | tf_op jit(solution)/shard_map/all_to_all | solution.py:99
  266.0 4.6 %fusion.12 = f32[16,1,4096]{2,1,0:T(1,128)S(1)} fusion(f32[16,16,1]{1,2,0:T(1,128)S(1)} %copy.15, bf16[16,16,4096]{2,1,0:T(8,128)(2,1)} %all-to-all-done.1), kind=kOutput, calls=%fused_computation.21 | convolution fusion | flops 12582912 | bytes 2360320 | tf_op jit(solution)/shard_map/td,dtk->tk/dot_general | solution.py:100
  270.5 0.0 copy-done.4
  270.6 0.2 fusion.54
  270.7 42.1 %collective-permute-start = (bf16[1,16,4096]{2,1,0:T(8,128)(2,1)S(1)}, bf16[1,16,4096]{2,1,0:T(8,128)(2,1)S(1)}, u32[]{:S(2)}, u32[]{:S(2)}) collective-permute-start(bf16[1,16,4096]{2,1,0:T(8,128)(2,1)S(1)} %fusion.54), channel_id=1, source_target_pairs={{240,0},{0,16},{16,32},{32,48},{48,64},{64,80},{80,96},{96,112},{1... | collective-permute-start | bytes 393224 | tf_op jit(solution)/shard_map/ppermute | solution.py:18
  312.8 5.1 %collective-permute-done = bf16[1,16,4096]{2,1,0:T(8,128)(2,1)S(1)} collective-permute-done((bf16[1,16,4096]{2,1,0:T(8,128)(2,1)S(1)}, bf16[1,16,4096]{2,1,0:T(8,128)(2,1)S(1)}, u32[]{:S(2)}, u32[]{:S(2)}) %collective-permute-start) | collective-permute-done | bytes 131104 | tf_op jit(solution)/shard_map/ppermute | solution.py:18
  318.0 0.7 copy.24
  (12 shorter events, 0.1 us)
Async XLA Ops:
  6.5 216.6 %copy-start = (bf16[1,384,4096]{2,1,0:T(8,128)(2,1)S(1)}, bf16[1,384,4096]{2,1,0:T(8,128)(2,1)}, u32[]{:S(2)}) copy-start(bf16[1,384,4096]{2,1,0:T(8,128)(2,1)} %param.17) | copy-start | bytes 9437188
  6.5 85.5 %copy-start.10 = (bf16[1,256,256]{2,1,0:T(8,128)(2,1)S(1)}, bf16[1,256,256]{2,1,0:T(8,128)(2,1)}, u32[]{:S(2)}) copy-start(bf16[1,256,256]{2,1,0:T(8,128)(2,1)} %param.11) | copy-start | bytes 393220
  6.5 83.1 %all-gather.3.cloned.1.call-start = ((), (), s32[]{:S(2)}) async-start(), calls=%async_computation.4 | async-start | bytes 4456448 | tf_op jit(solution)/shard_map/all_gather | solution.py:36
  7.3 176.0 %reduce-scatter.2.cloned.1.call-start = ((), (), s32[]{:S(2)}) async-start(), calls=%async_computation.3 | async-start | bytes 2228224 | tf_op jit(solution)/shard_map/reduce_scatter | solution.py:69
  89.7 2.5 copy-start.8
  96.1 1.6 copy-start.1
  97.1 86.2 %copy-start.3 = (bf16[1,16,4096]{2,1,0:T(8,128)(2,1)S(1)}, bf16[1,16,4096]{2,1,0:T(8,128)(2,1)}, u32[]{:S(2)}) copy-start(bf16[1,16,4096]{2,1,0:T(8,128)(2,1)} %param.10) | copy-start | bytes 393220
  97.1 87.4 %copy-start.5 = (f32[1,4096]{1,0:T(1,128)S(1)}, f32[1,4096]{1,0:T(1,128)}, u32[]{:S(2)}) copy-start(f32[1,4096]{1,0:T(1,128)} %param.14) | copy-start | bytes 49156
  183.3 37.8 %copy-start.9 = (bf16[1,4096,384]{2,1,0:T(8,128)(2,1)S(1)}, bf16[1,4096,384]{2,1,0:T(8,128)(2,1)}, u32[]{:S(2)}) copy-start(bf16[1,4096,384]{2,1,0:T(8,128)(2,1)} %param.15) | copy-start | bytes 9437188
  219.8 1.3 copy-start.2
  229.5 7.2 %copy-start.6 = (f32[1,256,2]{1,2,0:T(2,128)S(1)}, f32[1,256,2]{1,2,0:T(2,128)}, u32[]{:S(2)}) copy-start(f32[1,256,2]{1,2,0:T(2,128)} %param.19) | copy-start | bytes 6148
  229.5 7.3 %copy-start.7 = (s32[1,256,2]{1,2,0:T(2,128)S(1)}, s32[1,256,2]{1,2,0:T(2,128)}, u32[]{:S(2)}) copy-start(s32[1,256,2]{1,2,0:T(2,128)} %param.18) | copy-start | bytes 6148
  229.5 41.0 %copy-start.4 = (bf16[16,4096]{1,0:T(8,128)(2,1)S(1)}, bf16[16,4096]{1,0:T(8,128)(2,1)}, u32[]{:S(2)}) copy-start(bf16[16,4096]{1,0:T(8,128)(2,1)} %reduce-scatter.2.cloned.1.call-done) | copy-start | bytes 393220
  229.5 36.5 %all-to-all-start.1 = ((bf16[16,16,4096]{2,1,0:T(8,128)(2,1)}), bf16[16,16,4096]{2,1,0:T(8,128)(2,1)}, u32[]{:S(2)}, u32[]{:S(2)}) async-start(bf16[16,16,4096]{2,1,0:T(8,128)(2,1)} %bitcast.75), calls=%async_computation.2 | async-start | bytes 4194304 | tf_op jit(solution)/shard_map/all_to_all | solution.py:99
  270.7 47.2 %collective-permute-start = (bf16[1,16,4096]{2,1,0:T(8,128)(2,1)S(1)}, bf16[1,16,4096]{2,1,0:T(8,128)(2,1)S(1)}, u32[]{:S(2)}, u32[]{:S(2)}) collective-permute-start(bf16[1,16,4096]{2,1,0:T(8,128)(2,1)S(1)} %fusion.54), channel_id=1, source_target_pairs={{240,0},{0,16},{16,32},{32,48},{48,64},{64,80},{80,96},{96,112},{1... | collective-permute-start | bytes 393224 | tf_op jit(solution)/shard_map/ppermute | solution.py:18
Sparse Core Ops, SparseCore 0:
  10.0 79.6 all-gather.2
  99.9 83.3 reduce-scatter.1
where the time goes:
time: 326 us; the launch traced here: 325 us
  waiting for transfers between devices  201 us (62%)
  starting transfers between devices  49.3 us (15%)
  blocking collectives  34 us (10%)
  matrix products  21.1 us (6%)
  between operations  13.6 us (4%)
  other arithmetic  3.66 us (1%)
    reduce_scatter x1, waiting for transfers between devices, body(): lax.psum_scatter(jnp.dot(heads, proj_out, preferred_element_type=jnp.floa...  83.5 us
    all_gather x1, waiting for transfers between devices, body(): piece = lax.all_gather(keyvals[0], 'expert', axis=0, tiled=True)  82.3 us
    ppermute x1, starting transfers between devices, shifted(): return lax.ppermute(block, axis, route)  42.1 us
    all_to_all x1, blocking collectives, body(): lax.all_to_all(outgoing_rows, 'expert', split_axis=0, concat_axis=0, tile...  34 us
    all_to_all x1, waiting for transfers between devices, body(): lax.all_to_all(computed, 'expert', split_axis=0, concat_axis=0, tiled=True)  29 us
    all_to_all x1, starting transfers between devices, body(): lax.all_to_all(computed, 'expert', split_axis=0, concat_axis=0, tiled=True)  7.17 us
  transfers between devices with their start and end apart: 4, of which 4 were waited for; matrix products, arithmetic and copies ran while one was open for 0% of the time, Pallas kernels for 0%

commit v1 on v0

--- a/solution.py
+++ b/solution.py
@@ -33,7 +33,9 @@
     group = QHEADS // KVHEADS
     scale = 1.0 / math.sqrt(HD)
     query_pos = CTX - MB + jnp.arange(MB, dtype=jnp.int32)
-    piece = lax.all_gather(keyvals[0], "expert", axis=0, tiled=True)
+    piece = jnp.concatenate(
+        lax.all_to_all(jnp.stack([keyvals[0]] * lax.axis_size("expert")), "expert", 0, 0), axis=0
+    )
     tops = jnp.full((heads_here, MB), -1e30, jnp.float32)
     totals = jnp.zeros((heads_here, MB), jnp.float32)
     sums = jnp.zeros((heads_here, MB, HD), jnp.float32)

time: 326 us -> 362 us (1.11)
  starting transfers between devices: 49.3 us -> 65.2 us
  waiting for transfers between devices: 201 us -> 213 us
  matrix products: 21.1 us -> 24.8 us
    all_gather x1 -> x0, waiting for transfers between devices: 82.3 us -> none  [body(): piece = lax.all_gather(keyvals[0], 'expert', axis=0, tiled=True)]
    all_to_all x0 -> x1, waiting for transfers between devices: none -> 61.5 us  [body(): lax.all_to_all(jnp.stack([keyvals[0]] * lax.axis_size('expert')), 'expert...]
    reduce_scatter x1, waiting for transfers between devices: 83.5 us -> 120 us  [body(): lax.psum_scatter(jnp.dot(heads, proj_out, preferred_element_type=jnp.floa...]
    all_to_all x0 -> x1, starting transfers between devices: none -> 11.7 us  [body(): lax.all_to_all(jnp.stack([keyvals[0]] * lax.axis_size('expert')), 'expert...]
    ppermute x1, starting transfers between devices: 42.1 us -> 46.3 us  [shifted(): return lax.ppermute(block, axis, route)]
where the time goes in v1:
time: 362 us; the launch traced here: 360 us
  waiting for transfers between devices  213 us (59%)
  starting transfers between devices  65.2 us (18%)
  blocking collectives  33.9 us (9%)
  matrix products  24.8 us (7%)
  between operations  13.6 us (4%)
  local copies, waits for them, and re-layouts  5.84 us (2%)
  other arithmetic  3.65 us (1%)
    reduce_scatter x1, waiting for transfers between devices, body(): lax.psum_scatter(jnp.dot(heads, proj_out, preferred_element_type=jnp.floa...  120 us
    all_to_all x1, waiting for transfers between devices, body(): lax.all_to_all(jnp.stack([keyvals[0]] * lax.axis_size('expert')), 'expert...  61.5 us
    ppermute x1, starting transfers between devices, shifted(): return lax.ppermute(block, axis, route)  46.3 us
    all_to_all x1, blocking collectives, body(): lax.all_to_all(outgoing_rows, 'expert', split_axis=0, concat_axis=0, tile...  33.9 us
    all_to_all x1, waiting for transfers between devices, body(): lax.all_to_all(computed, 'expert', split_axis=0, concat_axis=0, tiled=True)  29 us
    all_to_all x1, starting transfers between devices, body(): lax.all_to_all(jnp.stack([keyvals[0]] * lax.axis_size('expert')), 'expert...  11.7 us
  transfers between devices with their start and end apart: 4, of which 4 were waited for; matrix products, arithmetic and copies ran while one was open for 0% of the time, Pallas kernels for 0%

profile of v1, /device:TPU:8, one launch (start us, length us, event | category | flops | bytes accessed | tf_op | source)
XLA Modules:
  0.0 360.5 jit_solution(6107939913456682592)
XLA Ops:
  6.5 0.0 copy-start
  6.5 3.5 stack.17
  10.0 0.0 copy-start.9
  10.0 11.7 %all-to-all-start = ((bf16[16,256,512]{2,1,0:T(8,128)(2,1)}), bf16[16,256,512]{2,1,0:T(8,128)(2,1)}, u32[]{:S(2)}, u32[]{:S(2)}) async-start(bf16[16,256,512]{2,1,0:T(8,128)(2,1)} %stack.17), calls=%async_computation | async-start | bytes 8388608 | tf_op jit(solution)/shard_map/all_to_all | solution.py:37
  21.7 0.0 reduce-scatter.2.cloned.1.call-start
  21.8 61.5 %all-to-all-done = bf16[16,256,512]{2,1,0:T(8,128)(2,1)} async-done(((bf16[16,256,512]{2,1,0:T(8,128)(2,1)}), bf16[16,256,512]{2,1,0:T(8,128)(2,1)}, u32[]{:S(2)}, u32[]{:S(2)}) %all-to-all-start) | async-done | bytes 4194336 | tf_op jit(solution)/shard_map/all_to_all | solution.py:37
  83.2 0.0 copy-done.9
  83.3 2.1 select_reduce_fusion.1
  85.4 3.0 fusion.2
  88.4 1.1 fusion.4
  89.5 2.2 fusion.27
  91.8 0.0 copy-start.1
  91.8 2.4 fusion.33
  94.2 0.0 copy-start.3
  94.2 0.0 copy-start.5
  94.2 0.0 copy-done.1
  94.2 2.1 convolution_convert_fusion.1
  96.3 0.0 reduce-scatter.2.cloned.1.call-update
  96.4 120.4 %reduce-scatter.2.cloned.1.call-done = bf16[16,4096]{1,0:T(8,128)(2,1)} async-done(((bf16[256,4096]{1,0:T(8,128)(2,1)}), bf16[16,4096]{1,0:T(8,128)(2,1)}) %reduce-scatter.2.cloned.1.call-update) | async-done | bytes 131088 | tf_op jit(solution)/shard_map/reduce_scatter | solution.py:71
  216.8 0.0 copy-done.3
  216.8 0.0 copy-start.8
  216.8 1.2 multiply_reduce_fusion
  218.0 0.0 copy-done.5
  218.0 1.0 multiply_convert_fusion
  219.0 0.2 broadcast_in_dim.53
  219.2 33.9 %all_to_all.15 = bf16[16,16,4096]{2,1,0:T(8,128)(2,1)S(1)} all-to-all(bf16[16,16,4096]{2,1,0:T(8,128)(2,1)S(1)} %broadcast_in_dim.53), channel_id=1, replica_groups=mesh['section'=16,'expert'=16] {'expert'}, dimensions={0} | all-to-all | bytes 4194304 | tf_op jit(solution)/shard_map/all_to_all | solution.py:91
  253.2 0.0 copy-start.2
  253.2 1.3 copy-done.2
  254.5 0.0 copy-done.8
  254.5 2.1 fusion.9
  256.5 0.0 copy-done
  256.5 6.4 %convolution_convert_fusion = bf16[256,4096]{1,0:T(8,128)(2,1)} fusion(bf16[1,384,4096]{2,1,0:T(8,128)(2,1)S(1)} %copy-done, bf16[256,4096]{1,0:T(8,128)(2,1)} %bitcast.63, bf16[1,4096,384]{2,1,0:T(8,128)(2,1)} %param.16, f32[256,384]{1,0:T(8,128)} %fusion.9), kind=kOutput, calls=%fused_computation.4 | convolution fusion | flops 1612251136 | bytes 10878976 | tf_op jit(solution)/shard_map/dot_general | solution.py:97
  262.9 0.0 copy-start.6
  262.9 0.0 copy-start.7
  262.9 0.0 copy-start.4
  262.9 7.2 %all-to-all-start.2 = ((bf16[16,16,4096]{2,1,0:T(8,128)(2,1)}), bf16[16,16,4096]{2,1,0:T(8,128)(2,1)}, u32[]{:S(2)}, u32[]{:S(2)}) async-start(bf16[16,16,4096]{2,1,0:T(8,128)(2,1)} %bitcast.61), calls=%async_computation.3 | async-start | bytes 4194304 | tf_op jit(solution)/shard_map/all_to_all | solution.py:101
  270.1 0.0 copy-done.6
  270.1 0.1 fusion.58
  270.2 0.0 copy-done.7
  270.2 0.1 fusion.57
  270.3 0.1 copy.15
  270.4 29.0 %all-to-all-done.2 = bf16[16,16,4096]{2,1,0:T(8,128)(2,1)} async-done(((bf16[16,16,4096]{2,1,0:T(8,128)(2,1)}), bf16[16,16,4096]{2,1,0:T(8,128)(2,1)}, u32[]{:S(2)}, u32[]{:S(2)}) %all-to-all-start.2) | async-done | bytes 2097184 | tf_op jit(solution)/shard_map/all_to_all | solution.py:101
  299.4 4.6 %fusion.12 = f32[16,1,4096]{2,1,0:T(1,128)S(1)} fusion(f32[16,16,1]{1,2,0:T(1,128)S(1)} %copy.15, bf16[16,16,4096]{2,1,0:T(8,128)(2,1)} %all-to-all-done.2), kind=kOutput, calls=%fused_computation.21 | convolution fusion | flops 12582912 | bytes 2360320 | tf_op jit(solution)/shard_map/td,dtk->tk/dot_general | solution.py:102
  304.0 0.0 copy-done.4
  304.0 0.2 fusion.50
  304.1 46.3 %collective-permute-start = (bf16[1,16,4096]{2,1,0:T(8,128)(2,1)S(1)}, bf16[1,16,4096]{2,1,0:T(8,128)(2,1)S(1)}, u32[]{:S(2)}, u32[]{:S(2)}) collective-permute-start(bf16[1,16,4096]{2,1,0:T(8,128)(2,1)S(1)} %fusion.50), channel_id=1, source_target_pairs={{240,0},{0,16},{16,32},{32,48},{48,64},{64,80},{80,96},{96,112},{1... | collective-permute-start | bytes 393224 | tf_op jit(solution)/shard_map/ppermute | solution.py:18
  350.4 2.5 collective-permute-done
  353.0 0.7 copy.24
  (10 shorter events, 0.1 us)
Async XLA Ops:
  6.5 250.0 %copy-start = (bf16[1,384,4096]{2,1,0:T(8,128)(2,1)S(1)}, bf16[1,384,4096]{2,1,0:T(8,128)(2,1)}, u32[]{:S(2)}) copy-start(bf16[1,384,4096]{2,1,0:T(8,128)(2,1)} %param.17) | copy-start | bytes 9437188
  10.0 73.2 %copy-start.9 = (bf16[1,256,256]{2,1,0:T(8,128)(2,1)S(1)}, bf16[1,256,256]{2,1,0:T(8,128)(2,1)}, u32[]{:S(2)}) copy-start(bf16[1,256,256]{2,1,0:T(8,128)(2,1)} %param.11) | copy-start | bytes 393220
  10.0 73.2 %all-to-all-start = ((bf16[16,256,512]{2,1,0:T(8,128)(2,1)}), bf16[16,256,512]{2,1,0:T(8,128)(2,1)}, u32[]{:S(2)}, u32[]{:S(2)}) async-start(bf16[16,256,512]{2,1,0:T(8,128)(2,1)} %stack.17), calls=%async_computation | async-start | bytes 8388608 | tf_op jit(solution)/shard_map/all_to_all | solution.py:37
  21.7 195.1 %reduce-scatter.2.cloned.1.call-start = ((), (), s32[]{:S(2)}) async-start(), calls=%async_computation.4 | async-start | bytes 2228224 | tf_op jit(solution)/shard_map/reduce_scatter | solution.py:71
  91.8 2.5 copy-start.1
  94.2 122.6 %copy-start.3 = (bf16[1,16,4096]{2,1,0:T(8,128)(2,1)S(1)}, bf16[1,16,4096]{2,1,0:T(8,128)(2,1)}, u32[]{:S(2)}) copy-start(bf16[1,16,4096]{2,1,0:T(8,128)(2,1)} %param.10) | copy-start | bytes 393220
  94.2 123.8 %copy-start.5 = (f32[1,4096]{1,0:T(1,128)S(1)}, f32[1,4096]{1,0:T(1,128)}, u32[]{:S(2)}) copy-start(f32[1,4096]{1,0:T(1,128)} %param.14) | copy-start | bytes 49156
  216.8 37.7 %copy-start.8 = (bf16[1,4096,384]{2,1,0:T(8,128)(2,1)S(1)}, bf16[1,4096,384]{2,1,0:T(8,128)(2,1)}, u32[]{:S(2)}) copy-start(bf16[1,4096,384]{2,1,0:T(8,128)(2,1)} %param.15) | copy-start | bytes 9437188
  253.2 1.3 copy-start.2
  262.9 7.2 %copy-start.6 = (f32[1,256,2]{1,2,0:T(2,128)S(1)}, f32[1,256,2]{1,2,0:T(2,128)}, u32[]{:S(2)}) copy-start(f32[1,256,2]{1,2,0:T(2,128)} %param.19) | copy-start | bytes 6148
  262.9 7.3 %copy-start.7 = (s32[1,256,2]{1,2,0:T(2,128)S(1)}, s32[1,256,2]{1,2,0:T(2,128)}, u32[]{:S(2)}) copy-start(s32[1,256,2]{1,2,0:T(2,128)} %param.18) | copy-start | bytes 6148
  262.9 41.1 %copy-start.4 = (bf16[16,4096]{1,0:T(8,128)(2,1)S(1)}, bf16[16,4096]{1,0:T(8,128)(2,1)}, u32[]{:S(2)}) copy-start(bf16[16,4096]{1,0:T(8,128)(2,1)} %reduce-scatter.2.cloned.1.call-done) | copy-start | bytes 393220
  262.9 36.5 %all-to-all-start.2 = ((bf16[16,16,4096]{2,1,0:T(8,128)(2,1)}), bf16[16,16,4096]{2,1,0:T(8,128)(2,1)}, u32[]{:S(2)}, u32[]{:S(2)}) async-start(bf16[16,16,4096]{2,1,0:T(8,128)(2,1)} %bitcast.61), calls=%async_computation.3 | async-start | bytes 4194304 | tf_op jit(solution)/shard_map/all_to_all | solution.py:101
  304.1 48.8 %collective-permute-start = (bf16[1,16,4096]{2,1,0:T(8,128)(2,1)S(1)}, bf16[1,16,4096]{2,1,0:T(8,128)(2,1)S(1)}, u32[]{:S(2)}, u32[]{:S(2)}) collective-permute-start(bf16[1,16,4096]{2,1,0:T(8,128)(2,1)S(1)} %fusion.50), channel_id=1, source_target_pairs={{240,0},{0,16},{16,32},{32,48},{48,64},{64,80},{80,96},{96,112},{1... | collective-permute-start | bytes 393224 | tf_op jit(solution)/shard_map/ppermute | solution.py:18
Sparse Core Ops, SparseCore 0:
  96.5 120.2 reduce-scatter.1
